TPU v7x, 256 devices: a whole 4x4x8 slice. The times are simulated.
256 devices in a mesh: blk: 8 (over x, y_hi), batch: 32 (over y_lo, z, core).
Axes of the slice: x: 4, y: 4 (y_hi: 2, y_lo: 2; y = y_hi * 2 + y_lo), z: 8, core: 2. Of those that a mesh axis runs over, the one named last changes fastest.
Arguments:
- frame_one: bfloat16 [32, 4096, 128], P('batch', 'blk'), may hold values from -40 to 40
- frame_two: bfloat16 [32, 4096, 128], P('batch', 'blk'), may hold values from -40 to 40
- encoder_weight: bfloat16 [128, 256], replicated, may hold values from -0.5 to 0.5
- flow_grad: float32 [32, 2, 4096], P('batch', None, 'blk'), may hold values from -6 to 6
Outputs:
- flow: float32 [32, 2, 4096], P('batch', None, 'blk')
- grad_w: float32 [128, 256], replicated
All inputs are finite; a program needn't handle non-finite values.
Results may differ from a plain program's by a relative error of at most 0.01.
Values may be sent and summed in bfloat16 or wider, within the bound.
No kernel may reach another device: no remote copies, remote signals or barrier semaphores. Data moves between devices by JAX's collectives and lax.ppermute only.
A program may use at most 64 MiB of HBM per device.

v0:
```python
import jax
import jax.numpy as jnp
from jax import lax
from jax.sharding import PartitionSpec as P

WIDTH = 240


def grid_coords(start, count):
    position = start + jnp.arange(count, dtype=jnp.int32)
    col_coord = (position % WIDTH).astype(jnp.float32) / 64.0
    row_coord = (position // WIDTH).astype(jnp.float32) / 8.0
    return (col_coord, row_coord)


def body(frame_one, frame_two, encoder_weight, flow_grad):
    first_in = frame_one[0]
    second_in = frame_two[0]
    grad_col = flow_grad[0, 0]
    grad_row = flow_grad[0, 1]
    query_count = first_in.shape[0]
    channels = encoder_weight.shape[1]
    scaling = channels ** (-0.5)
    first_feat = jnp.dot(first_in, encoder_weight, preferred_element_type=jnp.float32).astype(
        jnp.bfloat16
    )
    second_feat = jnp.dot(second_in, encoder_weight, preferred_element_type=jnp.float32).astype(
        jnp.bfloat16
    )
    own_col, own_row = grid_coords(lax.axis_index("blk") * query_count, query_count)
    zero_rows = jnp.zeros((query_count,), jnp.float32)
    forward_run_max = jnp.full((query_count,), -jnp.inf, jnp.float32)
    forward_run_sum = zero_rows
    sum_col = zero_rows
    sum_row = zero_rows
    key_feat = lax.all_gather(second_feat, "blk", axis=0, tiled=True)
    logits = scaling * jnp.dot(first_feat, key_feat.T, preferred_element_type=jnp.float32)
    key_col, key_row = grid_coords(jnp.int32(0), key_feat.shape[0])
    new_max = jnp.max(logits, axis=1)
    rescale = jnp.exp(forward_run_max - new_max)
    expo = jnp.exp(logits - new_max[:, None])
    forward_run_sum = forward_run_sum * rescale + jnp.sum(expo, axis=1)
    sum_col = sum_col * rescale + jnp.sum(expo * key_col[None, :], axis=1)
    sum_row = sum_row * rescale + jnp.sum(expo * key_row[None, :], axis=1)
    stats = (new_max, forward_run_sum, sum_col, sum_row)
    run_max, run_sum, sum_col, sum_row = stats
    mean_col = sum_col / run_sum
    mean_row = sum_row / run_sum
    inner = grad_col * mean_col + grad_row * mean_row
    flow = jnp.stack([mean_col - own_col, mean_row - own_row])[None]
    key_feat = lax.all_gather(second_feat, "blk", axis=0, tiled=True)
    logits = scaling * jnp.dot(first_feat, key_feat.T, preferred_element_type=jnp.float32)
    probs = jnp.exp(logits - run_max[:, None]) / run_sum[:, None]
    key_col, key_row = grid_coords(jnp.int32(0), key_feat.shape[0])
    slope = (
        probs
        * (
            grad_col[:, None] * key_col[None, :]
            + grad_row[:, None] * key_row[None, :]
            - inner[:, None]
        )
    ).astype(jnp.bfloat16)
    first_accum = jnp.dot(slope, key_feat, preferred_element_type=jnp.float32)
    first_accum, slope_store = (first_accum, slope)
    delta_one = (scaling * first_accum).astype(jnp.bfloat16)
    local_grad = jnp.dot(first_in.T, delta_one, preferred_element_type=jnp.float32)
    delta_two = lax.psum_scatter(
        scaling * jnp.dot(slope_store.T, first_feat, preferred_element_type=jnp.float32),
        "blk",
        scatter_dimension=0,
        tiled=True,
    )
    second_term = jnp.dot(
        second_in.astype(jnp.float32).T,
        delta_two,
        precision=lax.Precision.HIGHEST,
        preferred_element_type=jnp.float32,
    )
    local_grad = local_grad + second_term
    grad_w = lax.psum(local_grad, ("blk", "batch"))
    return (flow, grad_w)


def solution(mesh):
    placed = (P("batch", "blk", None), P("batch", "blk", None), P(), P("batch", None, "blk"))
    return jax.shard_map(
        body, mesh=mesh, in_specs=placed, out_specs=(P("batch", None, "blk"), P()), check_vma=False
    )
```

profile of v0, /device:TPU:2, one launch (start us, length us, event | category | flops | bytes accessed | tf_op | source)
XLA Modules:
  0.0 437.6 jit_solution(4563758125745906845)
XLA Ops:
  7.2 0.0 copy-start
  7.2 0.0 all-gather.2.cloned.1.call-start
  7.2 1.8 convolution_convert_fusion
  9.1 0.0 all-gather.2.cloned.1.call-update
  9.1 0.0 reduce-scatter.2.cloned.1.call-start
  9.2 0.8 fusion.24
  9.9 0.0 copy-done
  9.9 1.0 convolution_convert_fusion.1
  11.0 62.5 %all-gather.2.cloned.1.call-done = bf16[4096,256]{1,0:T(8,128)(2,1)} async-done(((bf16[512,256]{1,0:T(8,128)(2,1)}), bf16[4096,256]{1,0:T(8,128)(2,1)}) %all-gather.2.cloned.1.call-update) | async-done | bytes 2097168 | tf_op jit(solution)/shard_map/all_gather | solution.py:36
  73.5 3.0 multiply_reduce_fusion.2
  76.5 3.1 multiply_reduce_fusion.1
  79.6 4.2 multiply_convert_fusion
  83.8 0.0 copy-start.1
  83.8 1.9 copy-done.1
  85.7 0.0 copy-start.2
  85.7 3.3 convolution_multiply_fusion
  89.0 0.0 copy-start.3
  89.0 0.0 reduce-scatter.2.cloned.1.call-update
  89.0 0.0 all-reduce.2.cloned.1.call-start
  89.1 0.0 copy-done.2
  89.1 3.7 fusion.2
  92.9 85.5 %reduce-scatter.2.cloned.1.call-done = f32[512,256]{1,0:T(8,128)} async-done(((f32[4096,256]{1,0:T(8,128)}), f32[512,256]{1,0:T(8,128)}) %reduce-scatter.2.cloned.1.call-update) | async-done | bytes 524304 | tf_op jit(solution)/shard_map/reduce_scatter | solution.py:67
  178.4 0.0 copy-done.3
  178.4 2.3 fusion.1
  180.7 0.0 all-reduce.2.cloned.1.call-update
  180.7 0.6 maximum_bitcast_fusion
  181.3 248.1 %all-reduce.2.cloned.1.call-done = f32[128,256]{0,1:T(8,128)} async-done(((f32[128,256]{0,1:T(8,128)}), f32[128,256]{0,1:T(8,128)}) %all-reduce.2.cloned.1.call-update) | async-done | bytes 131088 | tf_op jit(solution)/shard_map/psum | solution.py:80
  429.4 1.7 copy.6
  (4 shorter events, 0.1 us)
Async XLA Ops:
  7.2 2.8 copy-start
  7.2 66.3 %all-gather.2.cloned.1.call-start = ((), (), s32[]{:S(2)}) async-start(), calls=%async_computation.1 | async-start | bytes 2359296 | tf_op jit(solution)/shard_map/all_gather | solution.py:36
  9.1 169.3 %reduce-scatter.2.cloned.1.call-start = ((), (), s32[]{:S(2)}) async-start(), calls=%async_computation.2 | async-start | bytes 4718592 | tf_op jit(solution)/shard_map/reduce_scatter | solution.py:67
  83.8 1.9 copy-start.1
  85.7 3.4 copy-start.2
  89.0 89.4 %copy-start.3 = (bf16[1,512,128]{2,1,0:T(8,128)(2,1)S(1)}, bf16[1,512,128]{2,1,0:T(8,128)(2,1)}, u32[]{:S(2)}) copy-start(bf16[1,512,128]{2,1,0:T(8,128)(2,1)} %param.5) | copy-start | bytes 393220
  89.0 340.4 %all-reduce.2.cloned.1.call-start = ((), (), s32[]{:S(2)}) async-start(), calls=%async_computation.3 | async-start | bytes 262144 | tf_op jit(solution)/shard_map/psum | solution.py:80
Sparse Core Ops, SparseCore 0:
  10.6 62.8 all-gather.1
  89.1 89.2 reduce-scatter.1
  184.5 244.9 all-reduce.1
where the time goes:
time: 438 us
  waiting for transfers between devices  396 us (90%)
  matrix products  15.1 us (3%)
  between operations  13.8 us (3%)
  other arithmetic  7.96 us (2%)
  local copies, waits for them, and re-layouts  4.38 us (1%)
    psum x1, waiting for transfers between devices, body(): grad_w = lax.psum(local_grad, ('blk', 'batch'))  248 us
    reduce_scatter x1, waiting for transfers between devices, body(): lax.psum_scatter(scaling * jnp.dot(slope_store.T, first_feat, preferred_e...  85.5 us
    all_gather x1, waiting for transfers between devices, body(): key_feat = lax.all_gather(second_feat, 'blk', axis=0, tiled=True)  62.5 us
  transfers between devices with their start and end apart: 3, of which 3 were waited for; matrix products, arithmetic and copies ran while one was open for 1% of the time, Pallas kernels for 0%

commit v1 on v0

--- a/solution.py
+++ b/solution.py
@@ -77,7 +77,7 @@
         preferred_element_type=jnp.float32,
     )
     local_grad = local_grad + second_term
-    grad_w = lax.psum(local_grad, ("blk", "batch"))
+    grad_w = jnp.sum(lax.all_gather(local_grad, ("blk", "batch")), axis=0)
     return (flow, grad_w)
 
 

time: 438 us -> 392 us (0.89)
  waiting for transfers between devices: 396 us -> 329 us
  local copies, waits for them, and re-layouts: 4.38 us -> 20.7 us
    psum x1 -> x0, waiting for transfers between devices: 248 us -> none  [body(): grad_w = lax.psum(local_grad, ('blk', 'batch'))]
    all_gather x0 -> x1, waiting for transfers between devices: none -> 181 us  [body(): grad_w = jnp.sum(lax.all_gather(local_grad, ('blk', 'batch')), axis=0)]
    unnamed x9 -> x12, local copies, waits for them, and re-layouts: 3.61 us -> 19.9 us
  transfers between devices with their start and end apart: 3 -> 3, of which waited for: 3 -> 3; matrix products, arithmetic and copies ran while one was open for 1% -> 2% of each run, Pallas kernels for 0% -> 0%
where the time goes in v1:
time: 392 us; the launch traced here: 390 us
  waiting for transfers between devices  329 us (84%)
  local copies, waits for them, and re-layouts  20.7 us (5%)
  matrix products  15.1 us (4%)
  between operations  13.8 us (4%)
  other arithmetic  12 us (3%)
    all_gather x1, waiting for transfers between devices, body(): grad_w = jnp.sum(lax.all_gather(local_grad, ('blk', 'batch')), axis=0)  181 us
    reduce_scatter x1, waiting for transfers between devices, body(): lax.psum_scatter(scaling * jnp.dot(slope_store.T, first_feat, preferred_e...  85.6 us
    all_gather x1, waiting for transfers between devices, body(): key_feat = lax.all_gather(second_feat, 'blk', axis=0, tiled=True)  62.5 us
    unnamed x12, local copies, waits for them, and re-layouts  19.9 us
  transfers between devices with their start and end apart: 3, of which 3 were waited for; matrix products, arithmetic and copies ran while one was open for 2% of the time, Pallas kernels for 0%

profile of v1, /device:TPU:2, one launch (start us, length us, event | category | flops | bytes accessed | tf_op | source)
XLA Modules:
  0.0 390.4 jit_solution(12148507394453188477)
XLA Ops:
  7.2 0.0 copy-start
  7.2 0.0 all-gather.4.cloned.1.call-start
  7.2 1.8 convolution_convert_fusion
  9.1 0.0 all-gather.4.cloned.1.call-update
  9.1 0.0 reduce-scatter.2.cloned.1.call-start
  9.2 0.8 fusion.24
  9.9 0.0 copy-done
  9.9 1.0 convolution_convert_fusion.1
  11.0 62.5 %all-gather.4.cloned.1.call-done = bf16[4096,256]{1,0:T(8,128)(2,1)} async-done(((bf16[512,256]{1,0:T(8,128)(2,1)}), bf16[4096,256]{1,0:T(8,128)(2,1)}) %all-gather.4.cloned.1.call-update) | async-done | bytes 2097168 | tf_op jit(solution)/shard_map/all_gather | solution.py:36
  73.5 3.0 multiply_reduce_fusion.2
  76.5 3.1 multiply_reduce_fusion.1
  79.6 4.2 %multiply_convert_fusion = bf16[512,4096]{1,0:T(8,128)(2,1)S(1)} fusion(f32[512]{0:T(512)S(1)} %get-tuple-element.7, f32[512]{0:T(512)S(1)} %bitcast.36, f32[512]{0:T(512)S(1)} %bitcast.34, f32[512]{0:T(512)S(1)} %get-tuple-element.10, f32[4096]{0:T(1024)S(1)} %get-tuple-element.15, f32[4096]{0:T(1024)S(1)} %get-tuple-element.16, ...), kind=kLoop, calls=%fused_computation.1 | loop fusion | flops 18874368 | bytes 12625920 | tf_op jit(solution)/shard_map/convert_element_type | solution.py:62
  83.8 0.0 copy-start.2
  83.8 1.9 copy-done.2
  85.7 0.0 copy-start.3
  85.7 3.2 convolution_multiply_fusion
  89.0 0.0 copy-start.4
  89.0 0.0 reduce-scatter.2.cloned.1.call-update
  89.0 0.0 all-gather.6.cloned.1.call-start
  89.0 0.0 copy-done.3
  89.1 3.7 fusion.2
  92.8 85.6 %reduce-scatter.2.cloned.1.call-done = f32[512,256]{1,0:T(8,128)} async-done(((f32[4096,256]{1,0:T(8,128)}), f32[512,256]{1,0:T(8,128)}) %reduce-scatter.2.cloned.1.call-update) | async-done | bytes 524304 | tf_op jit(solution)/shard_map/reduce_scatter | solution.py:67
  178.4 0.0 copy-done.4
  178.4 2.3 fusion.1
  180.7 0.0 all-gather.6.cloned.1.call-update
  180.8 0.6 maximum_bitcast_fusion
  181.4 180.5 %all-gather.6.cloned.1.call-done = f32[32768,256]{0,1:T(8,128)} async-done(((f32[128,256]{0,1:T(8,128)}), f32[32768,256]{0,1:T(8,128)}) %all-gather.6.cloned.1.call-update) | async-done | bytes 33554448 | tf_op jit(solution)/shard_map/all_gather | solution.py:80
  361.9 17.2 %copy.7 = f32[32,8,256,128]{3,2,1,0:T(8,128)S(1)} copy(f32[32,8,256,128]{3,1,2,0:T(8,128)} %bitcast.32) | data formatting | bytes 67108864
  379.1 0.0 copy-start.1
  379.2 4.0 %bitcast_reduce_fusion = f32[128,256]{0,1:T(8,128)S(1)} fusion(f32[32,8,256,128]{3,2,1,0:T(8,128)S(1)} %copy.7), kind=kLoop, calls=%fused_computation | loop fusion | flops 8355840 | bytes 33685504 | tf_op jit(solution)/shard_map/reduce_sum | solution.py:80
  383.2 0.8 copy.6
  383.9 0.0 copy-done.1
  (4 shorter events, 0.1 us)
Async XLA Ops:
  7.2 2.8 copy-start
  7.2 66.3 %all-gather.4.cloned.1.call-start = ((), (), s32[]{:S(2)}) async-start(), calls=%async_computation.1 | async-start | bytes 2359296 | tf_op jit(solution)/shard_map/all_gather | solution.py:36
  9.1 169.3 %reduce-scatter.2.cloned.1.call-start = ((), (), s32[]{:S(2)}) async-start(), calls=%async_computation.2 | async-start | bytes 4718592 | tf_op jit(solution)/shard_map/reduce_scatter | solution.py:67
  83.8 1.9 copy-start.2
  85.7 3.3 copy-start.3
  89.0 89.4 %copy-start.4 = (bf16[1,512,128]{2,1,0:T(8,128)(2,1)S(1)}, bf16[1,512,128]{2,1,0:T(8,128)(2,1)}, u32[]{:S(2)}) copy-start(bf16[1,512,128]{2,1,0:T(8,128)(2,1)} %param.5) | copy-start | bytes 393220
  89.0 272.9 %all-gather.6.cloned.1.call-start = ((), (), s32[]{:S(2)}) async-start(), calls=%async_computation.3 | async-start | bytes 33685504 | tf_op jit(solution)/shard_map/all_gather | solution.py:80
  379.1 4.8 %copy-start.1 = (bf16[1,512,128]{2,1,0:T(8,128)(2,1)S(1)}, bf16[1,512,128]{2,1,0:T(8,128)(2,1)}, u32[]{:S(2)}) copy-start(bf16[1,512,128]{2,1,0:T(8,128)(2,1)} %param.4) | copy-start | bytes 393220
Sparse Core Ops, SparseCore 0:
  10.6 62.8 all-gather.3
  89.1 89.2 reduce-scatter.1
  182.8 179.0 all-gather.5
